TPU v7x, 512 devices: a whole 4x8x8 slice. The times are simulated.
512 devices in a mesh: tm: 16 (over z, y_hi), space: 32 (over x, y_lo, core).
Axes of the slice: x: 4, y: 8 (y_hi: 2, y_lo: 4; y = y_hi * 4 + y_lo), z: 8, core: 2. Of those that a mesh axis runs over, the one named last changes fastest.
Arguments:
- state: float32 [16, 5, 256, 32, 128], P('tm', None, 'space'), may hold values from -6 to 6
- base: float32 [16, 5, 256, 32, 128], P('tm', None, 'space'), may hold values from -6 to 6
- pseudo_step: float32 [256, 32, 128], P('space'), may hold values from 0.05 to 0.3
- eddy_visc: float32 [256, 32, 128], P('space'), may hold values from 0.02 to 0.2
- jacobians: float32 [3, 5, 5], replicated, may hold values from -2.5 to 2.5
- partner_radial: int32 [2, 256, 128], P(None, 'space'), may hold values from 0 to 127, each once within a row
- partner_instance: int32 [16, 2, 256, 128], P('tm', None, 'space'), may hold values from 0 to 15, as said below
Outputs:
- updated: float32 [16, 5, 256, 32, 128], P('tm', None, 'space')
Inputs may be any that keep to these rules, and one draw needn't show every extreme that they name: partner_radial[s, i, :] is a permutation of the radial indices 0..127: the partner cells on the opposite periodic face in the same axial plane. partner_instance[n, 0, i, k] = (n + L_i) mod 16 and partner_instance[n, 1, i, k] = (n - L_i) mod 16 for a lag L_i in 1..15 that depends only on the axial plane i.
All inputs are finite; a program needn't handle non-finite values.
Results may differ from a plain program's by a relative error of at most 0.00005.
Values sent between devices are 32-bit elements; how exact they have to be, the bound alone decides.
No kernel may reach another device: no remote copies, remote signals or barrier semaphores. Data moves between devices by JAX's collectives and lax.ppermute only.
A program may use at most 64 MiB of HBM per device.

v0:
```python
import math
import jax
import jax.numpy as jnp
from jax import lax
from jax.sharding import Mesh
from jax.sharding import PartitionSpec as P

SECTION_ALPHA = 0.5
PITCH_ANGLE = 2.0 * math.pi / 36.0
NYQUIST_DAMP = 2.0
Y_PARTS = 2


def extended_2(block, sides, width):
    for axis, dim in sides:
        count = lax.axis_size(axis)
        forward = [(i, i + 1) for i in range(count - 1)]
        backward = [(target, source) for source, target in forward]
        low = lax.ppermute(
            lax.slice_in_dim(block, block.shape[dim] - width, None, axis=dim), axis, forward
        )
        high = lax.ppermute(lax.slice_in_dim(block, 0, width, axis=dim), axis, backward)
        block = jnp.concatenate([low, block, high], axis=dim)
    return block


def time_weights(offset, count):
    offset = offset % count
    angle = math.pi * offset.astype(jnp.float32) / count
    parity = jnp.where(offset % 2 == 1, 1.0, -1.0).astype(jnp.float32)
    sine = jnp.where(offset == 0, 1.0, jnp.sin(angle))
    spectral = 0.5 * parity * jnp.cos(angle) / sine - NYQUIST_DAMP * parity / count
    return jnp.where(offset == 0, NYQUIST_DAMP / count, spectral)


def rotate_velocity(values, turn):
    cosine = math.cos(PITCH_ANGLE)
    sine = turn * math.sin(PITCH_ANGLE)
    second = values[:, 2]
    third = values[:, 3]
    return jnp.stack(
        [
            values[:, 0],
            values[:, 1],
            cosine * second - sine * third,
            sine * second + cosine * third,
            values[:, 4],
        ],
        axis=1,
    )


def section_spatial(state, eddy_visc, jacobians, up_i, down_i, low_ghost, high_ghost):
    up_j = jnp.concatenate([state[:, :, :, 1:], high_ghost[:, :, :, None]], axis=3)
    down_j = jnp.concatenate([low_ghost[:, :, :, None], state[:, :, :, :-1]], axis=3)
    zeros = jnp.zeros(state.shape[:4] + (1,), state.dtype)
    up_k = jnp.concatenate([state[..., 1:], zeros], axis=4)
    down_k = jnp.concatenate([zeros, state[..., :-1]], axis=4)
    diffs = [(up_i - down_i) * 0.5, (up_j - down_j) * 0.5, (up_k - down_k) * 0.5]
    flux = None
    for direction, diff in enumerate(diffs):
        for source in range(state.shape[1]):
            column = jacobians[direction, :, source].reshape((1, -1) + (1,) * (state.ndim - 2))
            term = column * diff[:, source : source + 1]
            flux = term if flux is None else flux + term
    laplace = up_i + down_i + up_j + down_j + up_k + down_k - 6.0 * state
    return flux - eddy_visc[None, None] * laplace


def per_device(state, base, pseudo_step, eddy_visc, jacobians, partner_radial, partner_instance):
    ring = lax.axis_size("tz")
    total_count = ring * Y_PARTS
    z = lax.axis_index("tz")
    y = lax.axis_index("ty")
    own = Y_PARTS * z + y
    partner = own + 1 - 2 * y
    swap = [(i, Y_PARTS - 1 - i) for i in range(Y_PARTS)]
    ring_ids = Y_PARTS * jnp.arange(ring, dtype=jnp.int32) + y
    pitch = state.shape[3]
    edge = pitch // 4
    inner = state[:, :, :, edge : pitch - edge]
    other = lax.ppermute(inner, "ty", swap)
    expand = (ring,) + (1,) * (inner.ndim - 1)
    own_weights = time_weights(ring_ids - own, total_count).reshape(expand)
    partner_weights = time_weights(ring_ids - partner, total_count).reshape(expand)
    contributions = own_weights * inner + partner_weights * other
    inner_term = lax.psum_scatter(contributions, "tz", scatter_dimension=0, tiled=True)
    outer = jnp.concatenate([state[:, :, :, :edge], state[:, :, :, pitch - edge :]], axis=3)
    held = lax.all_gather(outer, "tz", axis=0, tiled=True)
    targets = jnp.stack([own, partner])
    weights = time_weights(targets[:, None] - ring_ids[None, :], total_count)
    partial = jnp.sum(weights.reshape((2, ring) + (1,) * (held.ndim - 1)) * held[None], axis=1)
    faces = jnp.stack([held[:, :, :, -1, :], held[:, :, :, 0, :]], axis=0)
    radial_count = partner_radial.shape[2]
    radial_hot = (partner_radial[..., None] == jnp.arange(radial_count, dtype=jnp.int32)).astype(
        jnp.float32
    )
    remapped = jnp.einsum("szvir,sikr->szvik", faces, radial_hot, precision=lax.Precision.HIGHEST)
    shifts = (targets - own)[:, None, None, None]
    sources = (partner_instance[0][None] + shifts) % total_count
    instance_hot = (sources[..., None] == ring_ids).astype(jnp.float32)
    picked = jnp.sum(instance_hot[:, :, None] * jnp.moveaxis(remapped, 1, -1)[None], axis=-1)
    message = jnp.concatenate([partial[1].reshape(-1), picked[1].reshape(-1)])
    received = lax.ppermute(message, "ty", swap)
    split = partial[0].size
    outer_term = partial[:1] + received[:split].reshape((1,) + partial.shape[1:])
    ghosts = picked[0] + received[split:].reshape(picked.shape[1:])
    time_term = jnp.concatenate(
        [outer_term[:, :, :, :edge], inner_term, outer_term[:, :, :, edge:]], axis=3
    )
    low_ghost = rotate_velocity(ghosts[0][None], -1.0)
    high_ghost = rotate_velocity(ghosts[1][None], 1.0)
    extended = extended_2(state, (("space", 2),), 1)
    up_i = extended[:, :, 2:]
    down_i = extended[:, :, :-2]
    spatial = lax.optimization_barrier(
        section_spatial(state, eddy_visc, jacobians, up_i, down_i, low_ghost, high_ghost)
    )
    return base - SECTION_ALPHA * pseudo_step[None, None] * (spatial + time_term)


def solution(mesh):
    devices = mesh.devices
    cells = devices.shape[1]
    split_mesh = Mesh(
        devices.reshape(devices.shape[0] // Y_PARTS, Y_PARTS, cells), ("tz", "ty", "space")
    )
    time_axes = ("tz", "ty")
    return jax.shard_map(
        per_device,
        mesh=split_mesh,
        in_specs=(
            P(time_axes, None, "space", None, None),
            P(time_axes, None, "space", None, None),
            P("space", None, None),
            P("space", None, None),
            P(),
            P(None, "space", None),
            P(time_axes, None, "space", None),
        ),
        out_specs=P(time_axes, None, "space", None, None),
        check_vma=False,
    )
```

profile of v0, /device:TPU:2, one launch (start us, length us, event | category | flops | bytes accessed | tf_op | source)
XLA Modules:
  0.0 117.2 jit_solution(7916101641822765204)
XLA Ops:
  6.5 0.0 all-gather.2.cloned.1.call-start
  6.5 1.1 fusion.22
  7.6 0.7 pad_maximum_fusion.5
  8.4 0.0 all-gather.2.cloned.1.call-update
  8.4 0.0 reduce-scatter.2.cloned.1.call-start
  8.5 1.6 %fusion.20 = (f32[1,5,1,32,128]{4,3,2,1,0:T(8,128)}, f32[1,5,1,32,128]{4,3,2,1,0:T(8,128)}) fusion(f32[1,5,8,32,128]{4,3,2,1,0:T(8,128)} %param.7), kind=kLoop, calls=%fused_computation.113 | loop fusion | bytes 327680 | tf_op jit(solution)/shard_map/slice | solution.py:20
  10.1 4.9 %collective-permute-start = (f32[1,5,1,32,128]{4,3,2,1,0:T(8,128)}, f32[1,5,1,32,128]{4,3,2,1,0:T(8,128)}, u32[]{:S(2)}, u32[]{:S(2)}) collective-permute-start(f32[1,5,1,32,128]{4,3,2,1,0:T(8,128)} %get-tuple-element.42), channel_id=1, source_target_pairs={{1,0},{2,1},{3,2},{4,3},{5,4},{6,5},{7,6},{8,7},{9,8},{10,9},{11,1... | collective-permute-start | bytes 245768 | tf_op jit(solution)/shard_map/ppermute | solution.py:22
  15.0 0.0 copy-start.11
  15.0 1.9 %collective-permute-start.1 = (f32[1,5,1,32,128]{4,3,2,1,0:T(8,128)}, f32[1,5,1,32,128]{4,3,2,1,0:T(8,128)}, u32[]{:S(2)}, u32[]{:S(2)}) collective-permute-start(f32[1,5,1,32,128]{4,3,2,1,0:T(8,128)} %get-tuple-element.41), channel_id=1, source_target_pairs={{0,1},{1,2},{2,3},{3,4},{4,5},{5,6},{6,7},{7,8},{8,9},{9,10},{10,1... | collective-permute-start | bytes 245768 | tf_op jit(solution)/shard_map/ppermute | solution.py:19
  16.9 1.9 %slice_bitcast_fusion.16 = (f32[5,8,16,128]{3,2,1,0:T(8,128)}, f32[1,5,8,16,128]{4,3,2,1,0:T(8,128)}) fusion(f32[1,5,8,32,128]{4,3,2,1,0:T(8,128)} %param.7), kind=kLoop, calls=%fused_computation.111 | loop fusion | bytes 983040 | tf_op jit(solution)/shard_map/mul | solution.py:86
  18.8 5.3 %collective-permute-start.3 = (f32[1,5,8,16,128]{4,3,2,1,0:T(8,128)}, f32[1,5,8,16,128]{4,3,2,1,0:T(8,128)}, u32[]{:S(2)}, u32[]{:S(2)}) collective-permute-start(f32[1,5,8,16,128]{4,3,2,1,0:T(8,128)} %get-tuple-element.25), channel_id=1, source_target_pairs={{0,32},{32,0},{1,33},{33,1},{2,34},{34,2},{3,35},{35,3},{4,36},{36... | collective-permute-start | bytes 983048 | tf_op jit(solution)/shard_map/ppermute | solution.py:82
  24.2 0.1 broadcast_subtract_fusion
  24.2 0.0 copy-done
  24.2 0.2 fusion.23
  24.5 1.1 subtract_multiply_fusion
  25.6 0.1 subtract_select_fusion
  25.7 0.0 copy-done.11
  25.7 0.1 add_select_fusion.1
  25.8 0.7 compare_convert_fusion
  26.5 0.0 copy-done.10
  26.5 0.7 broadcast_multiply_fusion
  27.2 0.1 compare_select_fusion.15
  27.3 0.1 fusion.21
  27.4 7.7 %collective-permute-done.3 = f32[1,5,8,16,128]{4,3,2,1,0:T(8,128)} collective-permute-done((f32[1,5,8,16,128]{4,3,2,1,0:T(8,128)}, f32[1,5,8,16,128]{4,3,2,1,0:T(8,128)}, u32[]{:S(2)}, u32[]{:S(2)}) %collective-permute-start.3) | collective-permute-done | bytes 327712 | tf_op jit(solution)/shard_map/ppermute | solution.py:82
  35.1 0.0 copy-done.3
  35.1 2.9 %multiply_add_fusion = f32[8,5,8,16,128]{4,3,2,1,0:T(8,128)} fusion(f32[5,8,16,128]{3,2,1,0:T(8,128)} %bitcast.33, f32[8]{0:T(128)S(1)} %get-tuple-element.61, f32[5,8,16,128]{3,2,1,0:T(8,128)S(1)} %copy-done.3, f32[8]{0:T(128)S(1)} %get-tuple-element.62), kind=kLoop, calls=%fused_computation.1 | loop fusion | flops 1966080 | bytes 3276864 | tf_op jit(solution)/shard_map/add | solution.py:86
  38.0 0.0 reduce-scatter.2.cloned.1.call-update
  38.1 0.0 copy-done.8
  38.1 0.9 slice_reduce_fusion.14
  39.0 1.9 %slice_bitcast_fusion.4 = (f32[8,32,128]{2,1,0:T(8,128)S(1)}, f32[8,32,128]{2,1,0:T(8,128)S(1)}, f32[8,32,128]{2,1,0:T(8,128)}, f32[8,32,128]{2,1,0:T(8,128)}, f32[8,32,128]{2,1,0:T(8,128)}) fusion(f32[1,5,8,32,128]{4,3,2,1,0:T(8,128)} %subtract_multiply_fusion), kind=kLoop, calls=%fused_computation.30 | loop fusion | bytes 1310720 | tf_op jit(solution)/shard_map/mul | solution.py:64
  40.9 19.1 %all-gather.2.cloned.1.call-done = f32[8,5,8,16,128]{4,3,2,1,0:T(8,128)} async-done(((f32[1,5,8,16,128]{4,3,2,1,0:T(8,128)}), f32[8,5,8,16,128]{4,3,2,1,0:T(8,128)}) %all-gather.2.cloned.1.call-update) | async-done | bytes 2621456 | tf_op jit(solution)/shard_map/all_gather | solution.py:89
  60.0 2.2 %fusion.19 = (f32[8,5,8,1,128]{4,3,2,1,0:T(1,128)S(1)}, f32[8,5,8,1,128]{4,3,2,1,0:T(1,128)S(1)}) fusion(f32[8,5,8,16,128]{4,3,2,1,0:T(8,128)} %all-gather.2.cloned.1.call-done), kind=kLoop, calls=%fused_computation.112 | loop fusion | bytes 655360 | tf_op jit(solution)/shard_map/slice | solution.py:93
  62.1 0.1 copy_bitcast_fusion
  62.2 2.1 %convolution_bitcast_fusion = f32[2,5,8,128,8]{3,4,1,2,0:T(8,128)S(1)} fusion(s32[2,8,128]{2,1,0:T(8,128)} %param.12, f32[1,8,5,8,128]{4,1,2,3,0:T(8,128)S(1)} %get-tuple-element.59, f32[1,8,5,8,128]{4,1,2,3,0:T(8,128)S(1)} %get-tuple-element.60), kind=kOutput, calls=%fused_computation.2 | convolution fusion | flops 126173184 | bytes 663552 | tf_op jit(solution)/shard_map/szvir,sikr->szvik/dot_general | solution.py:98
  64.4 1.1 multiply_reduce_fusion.1
  65.5 0.4 multiply_reduce_fusion
  66.0 7.1 %collective-permute-start.2 = (f32[92160]{0:T(1024)S(1)}, f32[92160]{0:T(1024)S(1)}, u32[]{:S(2)}, u32[]{:S(2)}) collective-permute-start(f32[92160]{0:T(1024)S(1)} %pad_maximum_fusion.4), channel_id=1, source_target_pairs={{0,32},{32,0},{1,33},{33,1},{2,34},{34,2},{3,35},{35,3},{4,36},{36... | collective-permute-start | bytes 1105928 | tf_op jit(solution)/shard_map/ppermute | solution.py:104
  73.1 0.0 collective-permute-done
  73.1 0.0 collective-permute-done.1
  73.1 1.0 subtract_multiply_fusion.2
  74.1 0.0 copy-start.9
  74.3 0.1 slice_bitcast_fusion.14
  74.3 8.3 %collective-permute-done.2 = f32[92160]{0:T(1024)S(1)} collective-permute-done((f32[92160]{0:T(1024)S(1)}, f32[92160]{0:T(1024)S(1)}, u32[]{:S(2)}, u32[]{:S(2)}) %collective-permute-start.2) | collective-permute-done | bytes 368672 | tf_op jit(solution)/shard_map/ppermute | solution.py:104
  82.7 0.2 subtract_multiply_fusion.1
  82.9 0.1 slice_bitcast_fusion.9
  83.1 3.0 %multiply_subtract_fusion = f32[1,5,8,32,128]{4,3,2,1,0:T(8,128)} fusion(f32[1,5,8,32,128]{4,3,2,1,0:T(8,128)S(1)} %copy-done, f32[1,5,8,32,127]{4,3,2,1,0:T(8,128)S(1)} %get-tuple-element.48, f32[1,5,8,32,127]{4,3,2,1,0:T(8,128)S(1)} %get-tuple-element.47, f32[1,5,8,31,128]{4,3,2,1,0:T(8,128)S(1)} %get-tuple-element.44, ...), kind=kLoop, calls=%fused_computation.12 | loop fusion | flops 6881280 | bytes 6183212 | tf_op jit(solution)/shard_map/sub | solution.py:67
  86.2 22.1 %reduce-scatter.2.cloned.1.call-done = f32[1,5,8,16,128]{4,3,2,1,0:T(8,128)} async-done(((f32[8,5,8,16,128]{4,3,2,1,0:T(8,128)}), f32[1,5,8,16,128]{4,3,2,1,0:T(8,128)}) %reduce-scatter.2.cloned.1.call-update) | async-done | bytes 327696 | tf_op jit(solution)/shard_map/reduce_scatter | solution.py:87
  108.4 2.0 %fusion.3 = f32[1,5,8,32,128]{4,3,2,1,0:T(8,128)} fusion(f32[1,5,8,32,128]{4,3,2,1,0:T(8,128)S(1)} %copy-done.4, f32[1,5,8,32,128]{4,3,2,1,0:T(8,128)S(1)} %copy-done.2, f32[1,5,8,8,128]{4,3,2,1,0:T(8,128)S(1)} %get-tuple-element.50, f32[1,5,8,16,128]{4,3,2,1,0:T(8,128)} %reduce-scatter.2.cloned.1.call-done, f32[1,5,8,8,128]{4,3,2,1,0:T(8,128)S(1)} %get-tuple-element.49, ...), kind=kLoop, calls=%fused_computation.11 | loop fusion | flops 819200 | bytes 2752512 | tf_op jit(solution)/shard_map/sub | solution.py:119
  (54 shorter events, 0.3 us)
Async XLA Ops:
  6.5 17.7 %copy-start = (f32[1,5,8,32,128]{4,3,2,1,0:T(8,128)S(1)}, f32[1,5,8,32,128]{4,3,2,1,0:T(8,128)}, u32[]{:S(2)}) copy-start(f32[1,5,8,32,128]{4,3,2,1,0:T(8,128)} %param.7) | copy-start | bytes 1966084
  6.5 53.4 %all-gather.2.cloned.1.call-start = ((), (), s32[]{:S(2)}) async-start(), calls=%async_computation.1 | async-start | bytes 2949120 | tf_op jit(solution)/shard_map/all_gather | solution.py:89
  8.4 100.0 %reduce-scatter.2.cloned.1.call-start = ((), (), s32[]{:S(2)}) async-start(), calls=%async_computation.2 | async-start | bytes 2949120 | tf_op jit(solution)/shard_map/reduce_scatter | solution.py:87
  10.1 63.0 %collective-permute-start = (f32[1,5,1,32,128]{4,3,2,1,0:T(8,128)}, f32[1,5,1,32,128]{4,3,2,1,0:T(8,128)}, u32[]{:S(2)}, u32[]{:S(2)}) collective-permute-start(f32[1,5,1,32,128]{4,3,2,1,0:T(8,128)} %get-tuple-element.42), channel_id=1, source_target_pairs={{1,0},{2,1},{3,2},{4,3},{5,4},{6,5},{7,6},{8,7},{9,8},{10,9},{11,1... | collective-permute-start | bytes 245768 | tf_op jit(solution)/shard_map/ppermute | solution.py:22
  15.0 10.7 %copy-start.11 = (s32[1,2,8,128]{3,2,1,0:T(8,128)S(1)}, s32[1,2,8,128]{3,2,1,0:T(8,128)}, u32[]{:S(2)}) copy-start(s32[1,2,8,128]{3,2,1,0:T(8,128)} %param.13) | copy-start | bytes 24580
  15.0 58.1 %collective-permute-start.1 = (f32[1,5,1,32,128]{4,3,2,1,0:T(8,128)}, f32[1,5,1,32,128]{4,3,2,1,0:T(8,128)}, u32[]{:S(2)}, u32[]{:S(2)}) collective-permute-start(f32[1,5,1,32,128]{4,3,2,1,0:T(8,128)} %get-tuple-element.41), channel_id=1, source_target_pairs={{0,1},{1,2},{2,3},{3,4},{4,5},{5,6},{6,7},{7,8},{8,9},{9,10},{10,1... | collective-permute-start | bytes 245768 | tf_op jit(solution)/shard_map/ppermute | solution.py:19
  18.8 7.7 %copy-start.10 = (f32[8,32,128]{2,1,0:T(8,128)S(1)}, f32[8,32,128]{2,1,0:T(8,128)}, u32[]{:S(2)}) copy-start(f32[8,32,128]{2,1,0:T(8,128)} %param.9) | copy-start | bytes 393220
  18.8 16.3 %collective-permute-start.3 = (f32[1,5,8,16,128]{4,3,2,1,0:T(8,128)}, f32[1,5,8,16,128]{4,3,2,1,0:T(8,128)}, u32[]{:S(2)}, u32[]{:S(2)}) collective-permute-start(f32[1,5,8,16,128]{4,3,2,1,0:T(8,128)} %get-tuple-element.25), channel_id=1, source_target_pairs={{0,32},{32,0},{1,33},{33,1},{2,34},{34,2},{3,35},{35,3},{4,36},{36... | collective-permute-start | bytes 983048 | tf_op jit(solution)/shard_map/ppermute | solution.py:82
  24.5 10.6 %copy-start.3 = (f32[5,8,16,128]{3,2,1,0:T(8,128)S(1)}, f32[5,8,16,128]{3,2,1,0:T(8,128)}, u32[]{:S(2)}) copy-start(f32[5,8,16,128]{3,2,1,0:T(8,128)} %get-tuple-element.24) | copy-start | bytes 983044
  35.1 3.0 %copy-start.8 = (f32[3,5,5]{2,0,1:T(4,128)S(1)}, f32[3,5,5]{2,0,1:T(4,128)}, u32[]{:S(2)}) copy-start(f32[3,5,5]{2,0,1:T(4,128)} %param.11) | copy-start | bytes 904
  60.0 5.5 %copy-start.1 = (f32[8,5,8,16,128]{4,3,2,1,0:T(8,128)S(1)}, f32[8,5,8,16,128]{4,3,2,1,0:T(8,128)}, u32[]{:S(2)}) copy-start(f32[8,5,8,16,128]{4,3,2,1,0:T(8,128)} %all-gather.2.cloned.1.call-done) | copy-start | bytes 7864324
  66.0 16.7 %collective-permute-start.2 = (f32[92160]{0:T(1024)S(1)}, f32[92160]{0:T(1024)S(1)}, u32[]{:S(2)}, u32[]{:S(2)}) collective-permute-start(f32[92160]{0:T(1024)S(1)} %pad_maximum_fusion.4), channel_id=1, source_target_pairs={{0,32},{32,0},{1,33},{33,1},{2,34},{34,2},{3,35},{35,3},{4,36},{36... | collective-permute-start | bytes 1105928 | tf_op jit(solution)/shard_map/ppermute | solution.py:104
  74.1 8.9 %copy-start.5 = (f32[8,32,128]{2,1,0:T(8,128)S(1)}, f32[8,32,128]{2,1,0:T(8,128)}, u32[]{:S(2)}) copy-start(f32[8,32,128]{2,1,0:T(8,128)} %get-tuple-element.38) | copy-start | bytes 393220
  74.1 8.9 %copy-start.6 = (f32[8,32,128]{2,1,0:T(8,128)S(1)}, f32[8,32,128]{2,1,0:T(8,128)}, u32[]{:S(2)}) copy-start(f32[8,32,128]{2,1,0:T(8,128)} %get-tuple-element.39) | copy-start | bytes 393220
  74.1 8.9 %copy-start.7 = (f32[8,32,128]{2,1,0:T(8,128)S(1)}, f32[8,32,128]{2,1,0:T(8,128)}, u32[]{:S(2)}) copy-start(f32[8,32,128]{2,1,0:T(8,128)} %get-tuple-element.40) | copy-start | bytes 393220
  74.1 8.9 %copy-start.9 = (f32[8,32,128]{2,1,0:T(8,128)S(1)}, f32[8,32,128]{2,1,0:T(8,128)}, u32[]{:S(2)}) copy-start(f32[8,32,128]{2,1,0:T(8,128)} %param.10) | copy-start | bytes 393220
  74.1 8.9 %copy-start.12 = (f32[5]{0:T(128)S(1)}, f32[5]{0:T(128)}, u32[]{:S(2)}) copy-start(f32[5]{0:T(128)} %get-tuple-element.8) | copy-start | bytes 64
  74.2 8.9 %copy-start.13 = (f32[5]{0:T(128)S(1)}, f32[5]{0:T(128)}, u32[]{:S(2)}) copy-start(f32[5]{0:T(128)} %get-tuple-element.9) | copy-start | bytes 64
  74.2 8.9 %copy-start.14 = (f32[5]{0:T(128)S(1)}, f32[5]{0:T(128)}, u32[]{:S(2)}) copy-start(f32[5]{0:T(128)} %get-tuple-element.10) | copy-start | bytes 64
  74.2 8.9 %copy-start.15 = (f32[5]{0:T(128)S(1)}, f32[5]{0:T(128)}, u32[]{:S(2)}) copy-start(f32[5]{0:T(128)} %get-tuple-element.11) | copy-start | bytes 64
  74.2 8.9 %copy-start.16 = (f32[5]{0:T(128)S(1)}, f32[5]{0:T(128)}, u32[]{:S(2)}) copy-start(f32[5]{0:T(128)} %get-tuple-element.12) | copy-start | bytes 64
  74.2 8.9 %copy-start.17 = (f32[5]{0:T(128)S(1)}, f32[5]{0:T(128)}, u32[]{:S(2)}) copy-start(f32[5]{0:T(128)} %get-tuple-element.13) | copy-start | bytes 64
  74.2 8.9 %copy-start.18 = (f32[5]{0:T(128)S(1)}, f32[5]{0:T(128)}, u32[]{:S(2)}) copy-start(f32[5]{0:T(128)} %get-tuple-element.14) | copy-start | bytes 64
  74.2 8.9 %copy-start.19 = (f32[5]{0:T(128)S(1)}, f32[5]{0:T(128)}, u32[]{:S(2)}) copy-start(f32[5]{0:T(128)} %get-tuple-element.15) | copy-start | bytes 64
  74.2 8.9 %copy-start.20 = (f32[5]{0:T(128)S(1)}, f32[5]{0:T(128)}, u32[]{:S(2)}) copy-start(f32[5]{0:T(128)} %get-tuple-element.16) | copy-start | bytes 64
  74.2 8.9 %copy-start.21 = (f32[5]{0:T(128)S(1)}, f32[5]{0:T(128)}, u32[]{:S(2)}) copy-start(f32[5]{0:T(128)} %get-tuple-element.17) | copy-start | bytes 64
  74.2 8.9 %copy-start.22 = (f32[5]{0:T(128)S(1)}, f32[5]{0:T(128)}, u32[]{:S(2)}) copy-start(f32[5]{0:T(128)} %get-tuple-element.18) | copy-start | bytes 64
  74.3 8.9 %copy-start.23 = (f32[5]{0:T(128)S(1)}, f32[5]{0:T(128)}, u32[]{:S(2)}) copy-start(f32[5]{0:T(128)} %get-tuple-element.19) | copy-start | bytes 64
  86.1 22.3 %copy-start.2 = (f32[1,5,8,32,128]{4,3,2,1,0:T(8,128)S(1)}, f32[1,5,8,32,128]{4,3,2,1,0:T(8,128)}, u32[]{:S(2)}) copy-start(f32[1,5,8,32,128]{4,3,2,1,0:T(8,128)} %multiply_subtract_fusion) | copy-start | bytes 1966084
  86.1 22.3 %copy-start.4 = (f32[1,5,8,32,128]{4,3,2,1,0:T(8,128)S(1)}, f32[1,5,8,32,128]{4,3,2,1,0:T(8,128)}, u32[]{:S(2)}) copy-start(f32[1,5,8,32,128]{4,3,2,1,0:T(8,128)} %param.8) | copy-start | bytes 1966084
Sparse Core Ops, SparseCore 0:
  9.4 50.4 all-gather.1
  62.8 45.4 reduce-scatter.1
where the time goes:
time: 118 us; the launch traced here: 117 us
  waiting for transfers between devices  57.3 us (49%)
  starting transfers between devices  19.3 us (16%)
  other arithmetic  14.4 us (12%)
  between operations  13.9 us (12%)
  local copies, waits for them, and re-layouts  10.3 us (9%)
  matrix products  2.13 us (2%)
    reduce_scatter x1, waiting for transfers between devices, per_device(): lax.psum_scatter(contributions, 'tz', scatter_dimension=0, tiled=True)  22.1 us
    all_gather x1, waiting for transfers between devices, per_device(): held = lax.all_gather(outer, 'tz', axis=0, tiled=True)  19.1 us
    ppermute x1, waiting for transfers between devices, per_device(): received = lax.ppermute(message, 'ty', swap)  8.32 us
    ppermute x1, waiting for transfers between devices, per_device(): other = lax.ppermute(inner, 'ty', swap)  7.71 us
    ppermute x1, starting transfers between devices, per_device(): received = lax.ppermute(message, 'ty', swap)  7.05 us
    ppermute x1, starting transfers between devices, per_device(): other = lax.ppermute(inner, 'ty', swap)  5.34 us
    ppermute x1, starting transfers between devices, extended_2(): lax.ppermute(lax.slice_in_dim(block, 0, width, axis=dim), axis, backward)  4.91 us
    sub x1, other arithmetic, section_spatial(): return flux - eddy_visc[None, None] * laplace  2.97 us
  transfers between devices with their start and end apart: 6, of which 4 were waited for; matrix products, arithmetic and copies ran while one was open for 19% of the time, Pallas kernels for 0%

commit v1 on v0

--- a/solution.py
+++ b/solution.py
@@ -9,6 +9,11 @@
 PITCH_ANGLE = 2.0 * math.pi / 36.0
 NYQUIST_DAMP = 2.0
 Y_PARTS = 2
+
+
+def exchange_gather(value, axis, dim):
+    sent = jnp.stack([value] * lax.axis_size(axis))
+    return jnp.concatenate(lax.all_to_all(sent, axis, 0, 0), axis=dim)
 
 
 def extended_2(block, sides, width):
@@ -86,7 +91,7 @@
     contributions = own_weights * inner + partner_weights * other
     inner_term = lax.psum_scatter(contributions, "tz", scatter_dimension=0, tiled=True)
     outer = jnp.concatenate([state[:, :, :, :edge], state[:, :, :, pitch - edge :]], axis=3)
-    held = lax.all_gather(outer, "tz", axis=0, tiled=True)
+    held = exchange_gather(outer, "tz", 0)
     targets = jnp.stack([own, partner])
     weights = time_weights(targets[:, None] - ring_ids[None, :], total_count)
     partial = jnp.sum(weights.reshape((2, ring) + (1,) * (held.ndim - 1)) * held[None], axis=1)

time: 118 us -> 126 us (1.068)
  the two profiles are of different devices: /device:TPU:2 before, /device:TPU:63 now
where the time goes in v1:
time: 126 us
  waiting for transfers between devices  61.8 us (49%)
  starting transfers between devices  24.1 us (19%)
  between operations  14 us (11%)
  local copies, waits for them, and re-layouts  12.3 us (10%)
  other arithmetic  11.8 us (9%)
  matrix products  1.43 us (1%)
    all_to_all x1, waiting for transfers between devices, exchange_gather(): return jnp.concatenate(lax.all_to_all(sent, axis, 0, 0), axis=dim)  34.3 us
    ppermute x1, waiting for transfers between devices, per_device(): received = lax.ppermute(message, 'ty', swap)  18.6 us
    all_to_all x1, starting transfers between devices, exchange_gather(): return jnp.concatenate(lax.all_to_all(sent, axis, 0, 0), axis=dim)  10.2 us
    ppermute x1, waiting for transfers between devices, per_device(): other = lax.ppermute(inner, 'ty', swap)  8.84 us
    ppermute x1, starting transfers between devices, per_device(): other = lax.ppermute(inner, 'ty', swap)  4.55 us
    ppermute x1, starting transfers between devices, per_device(): received = lax.ppermute(message, 'ty', swap)  4.45 us
    ppermute x1, starting transfers between devices, extended_2(): lax.ppermute(lax.slice_in_dim(block, 0, width, axis=dim), axis, backward)  3.49 us
    add x1, other arithmetic, per_device(): contributions = own_weights * inner + partner_weights * other  2.93 us
  transfers between devices with their start and end apart: 6, of which 3 were waited for; matrix products, arithmetic and copies ran while one was open for 15% of the time, Pallas kernels for 0%

profile of v1, /device:TPU:63, one launch (start us, length us, event | category | flops | bytes accessed | tf_op | source)
XLA Modules:
  0.0 125.5 jit_solution(15364141194878022095)
XLA Ops:
  6.5 1.0 fusion.21
  7.6 1.8 %stack.38 = f32[8,1,5,8,16,128]{5,4,3,2,1,0:T(8,128)} broadcast(f32[5,8,16,128]{3,2,1,0:T(8,128)S(1)} %maximum_bitcast_fusion), dimensions={2,3,4,5} | broadcast | bytes 2949120 | tf_op jit(solution)/shard_map/stack | solution.py:15
  9.4 10.2 %all-to-all-start = ((f32[8,1,5,8,16,128]{5,4,3,2,1,0:T(8,128)}), f32[8,1,5,8,16,128]{5,4,3,2,1,0:T(8,128)S(1)}, u32[]{:S(2)}, u32[]{:S(2)}) async-start(f32[8,1,5,8,16,128]{5,4,3,2,1,0:T(8,128)} %stack.38), calls=%async_computation | async-start | bytes 5242880 | tf_op jit(solution)/shard_map/all_to_all | solution.py:16
  19.6 0.0 reduce-scatter.2.cloned.1.call-start
  19.6 0.7 fusion.19
  20.3 3.5 %collective-permute-start = (f32[1,5,1,32,128]{4,3,2,1,0:T(8,128)}, f32[1,5,1,32,128]{4,3,2,1,0:T(8,128)}, u32[]{:S(2)}, u32[]{:S(2)}) collective-permute-start(f32[1,5,1,32,128]{4,3,2,1,0:T(8,128)} %get-tuple-element.42), channel_id=1, source_target_pairs={{1,0},{2,1},{3,2},{4,3},{5,4},{6,5},{7,6},{8,7},{9,8},{10,9},{11,1... | collective-permute-start | bytes 245768 | tf_op jit(solution)/shard_map/ppermute | solution.py:27
  23.8 1.4 %collective-permute-start.1 = (f32[1,5,1,32,128]{4,3,2,1,0:T(8,128)}, f32[1,5,1,32,128]{4,3,2,1,0:T(8,128)}, u32[]{:S(2)}, u32[]{:S(2)}) collective-permute-start(f32[1,5,1,32,128]{4,3,2,1,0:T(8,128)} %get-tuple-element.41), channel_id=1, source_target_pairs={{0,1},{1,2},{2,3},{3,4},{4,5},{5,6},{6,7},{7,8},{8,9},{9,10},{10,1... | collective-permute-start | bytes 245768 | tf_op jit(solution)/shard_map/ppermute | solution.py:24
  25.2 0.9 slice_bitcast_fusion.18
  26.1 4.6 %collective-permute-start.3 = (f32[1,5,8,16,128]{4,3,2,1,0:T(8,128)}, f32[1,5,8,16,128]{4,3,2,1,0:T(8,128)}, u32[]{:S(2)}, u32[]{:S(2)}) collective-permute-start(f32[1,5,8,16,128]{4,3,2,1,0:T(8,128)} %get-tuple-element.25), channel_id=1, source_target_pairs={{0,32},{32,0},{1,33},{33,1},{2,34},{34,2},{3,35},{35,3},{4,36},{36... | collective-permute-start | bytes 983048 | tf_op jit(solution)/shard_map/ppermute | solution.py:87
  30.7 0.1 broadcast_subtract_fusion
  30.8 0.2 fusion.22
  31.1 0.0 copy-start.5
  31.1 0.9 copy-done.3
  31.9 1.1 subtract_multiply_fusion
  33.1 0.1 subtract_select_fusion
  33.2 0.0 copy-done.17
  33.2 0.1 add_select_fusion.1
  33.3 0.7 compare_convert_fusion
  34.0 0.1 compare_select_fusion.15
  34.1 0.7 broadcast_multiply_fusion
  34.7 8.8 %collective-permute-done.3 = f32[1,5,8,16,128]{4,3,2,1,0:T(8,128)} collective-permute-done((f32[1,5,8,16,128]{4,3,2,1,0:T(8,128)}, f32[1,5,8,16,128]{4,3,2,1,0:T(8,128)}, u32[]{:S(2)}, u32[]{:S(2)}) %collective-permute-start.3) | collective-permute-done | bytes 327712 | tf_op jit(solution)/shard_map/ppermute | solution.py:87
  43.6 0.0 copy-done.7
  43.6 2.9 %multiply_add_fusion = f32[8,5,8,16,128]{4,3,2,1,0:T(8,128)} fusion(f32[5,8,16,128]{3,2,1,0:T(8,128)} %bitcast.36, f32[8]{0:T(128)S(1)} %get-tuple-element.59, f32[5,8,16,128]{3,2,1,0:T(8,128)S(1)} %copy-done.7, f32[8]{0:T(128)S(1)} %get-tuple-element.60), kind=kLoop, calls=%fused_computation.2 | loop fusion | flops 1966080 | bytes 3276864 | tf_op jit(solution)/shard_map/add | solution.py:91
  46.5 0.0 reduce-scatter.2.cloned.1.call-update
  46.6 0.9 slice_reduce_fusion.14
  47.4 1.9 %slice_bitcast_fusion.6 = (f32[8,32,128]{2,1,0:T(8,128)S(1)}, f32[8,32,128]{2,1,0:T(8,128)S(1)}, f32[8,32,128]{2,1,0:T(8,128)}, f32[8,32,128]{2,1,0:T(8,128)}, f32[8,32,128]{2,1,0:T(8,128)}) fusion(f32[1,5,8,32,128]{4,3,2,1,0:T(8,128)} %subtract_multiply_fusion), kind=kLoop, calls=%fused_computation.31 | loop fusion | bytes 1310720 | tf_op jit(solution)/shard_map/mul | solution.py:69
  49.4 1.2 fusion.20
  50.5 34.3 %all-to-all-done = f32[8,1,5,8,16,128]{5,4,3,2,1,0:T(8,128)S(1)} async-done(((f32[8,1,5,8,16,128]{5,4,3,2,1,0:T(8,128)}), f32[8,1,5,8,16,128]{5,4,3,2,1,0:T(8,128)S(1)}, u32[]{:S(2)}, u32[]{:S(2)}) %all-to-all-start) | async-done | bytes 2621472 | tf_op jit(solution)/shard_map/all_to_all | solution.py:16
  84.9 1.5 %copy.35 = f32[8,1,5,8,16,128]{5,0,2,3,4,1:T(8,128)S(1)} copy(f32[8,1,5,8,16,128]{5,4,3,2,1,0:T(8,128)S(1)} %all-to-all-done) | data formatting | bytes 5242880 | tf_op jit(solution)/shard_map/all_to_all | solution.py:16
  86.4 1.4 %convolution_bitcast_fusion = f32[2,5,8,128,8]{3,4,1,2,0:T(8,128)S(1)} fusion(s32[2,8,128]{2,1,0:T(8,128)S(1)} %copy-done.30, f32[1,8,5,8,128]{4,1,2,3,0:T(8,128)S(1)} %get-tuple-element.23, f32[1,8,5,8,128]{4,1,2,3,0:T(8,128)S(1)} %get-tuple-element.22), kind=kOutput, calls=%fused_computation.3 | convolution fusion | flops 126173184 | bytes 663552 | tf_op jit(solution)/shard_map/szvir,sikr->szvik/dot_general | solution.py:103
  87.9 0.2 multiply_reduce_fusion.1
  88.1 0.4 multiply_reduce_fusion
  88.6 4.4 %collective-permute-start.2 = (f32[92160]{0:T(1024)S(1)}, f32[92160]{0:T(1024)S(1)}, u32[]{:S(2)}, u32[]{:S(2)}) collective-permute-start(f32[92160]{0:T(1024)S(1)} %pad_maximum_fusion.4), channel_id=1, source_target_pairs={{0,32},{32,0},{1,33},{33,1},{2,34},{34,2},{3,35},{35,3},{4,36},{36... | collective-permute-start | bytes 1105928 | tf_op jit(solution)/shard_map/ppermute | solution.py:109
  93.1 0.0 collective-permute-done
  93.1 0.0 collective-permute-done.1
  93.1 1.0 subtract_multiply_fusion.2
  94.1 0.0 copy-start.6
  94.2 0.0 copy-start.15
  94.4 18.6 %collective-permute-done.2 = f32[92160]{0:T(1024)S(1)} collective-permute-done((f32[92160]{0:T(1024)S(1)}, f32[92160]{0:T(1024)S(1)}, u32[]{:S(2)}, u32[]{:S(2)}) %collective-permute-start.2) | collective-permute-done | bytes 368672 | tf_op jit(solution)/shard_map/ppermute | solution.py:109
  113.0 0.0 copy-done.1
  113.0 0.0 copy-done.2
  113.0 0.2 subtract_multiply_fusion.1
  113.4 2.1 %multiply_subtract_fusion = f32[1,5,8,32,128]{4,3,2,1,0:T(8,128)S(1)} fusion(f32[1,5,8,32,128]{4,3,2,1,0:T(8,128)S(1)} %copy-done, f32[1,5,8,32,127]{4,3,2,1,0:T(8,128)S(1)} %copy-done.6, f32[1,5,8,32,127]{4,3,2,1,0:T(8,128)S(1)} %copy-done.4, f32[1,5,8,31,128]{4,3,2,1,0:T(8,128)S(1)} %copy-done.2, f32[1,5,8,1,128]{4,3,2,1,0:T(1,128)S(1)} %bitcast.74, ...), kind=kLoop, calls=%fused_computation.13 | loop fusion | flops 6881280 | bytes 6183212 | tf_op jit(solution)/shard_map/sub | solution.py:72
  115.6 0.0 copy-start.8
  115.7 0.0 reduce-scatter.2.cloned.1.call-done
  115.7 0.0 copy-done.13
  115.7 0.9 copy-done.8
  116.7 2.0 %fusion.3 = f32[1,5,8,32,128]{4,3,2,1,0:T(8,128)} fusion(f32[1,5,8,32,128]{4,3,2,1,0:T(8,128)S(1)} %copy-done.8, f32[1,5,8,32,128]{4,3,2,1,0:T(8,128)S(1)} %multiply_subtract_fusion, f32[1,5,8,8,128]{4,3,2,1,0:T(8,128)S(1)} %get-tuple-element.50, f32[1,5,8,16,128]{4,3,2,1,0:T(8,128)} %reduce-scatter.2.cloned.1.call-done, ...), kind=kLoop, calls=%fused_computation.12 | loop fusion | flops 819200 | bytes 2752512 | tf_op jit(solution)/shard_map/sub | solution.py:124
  (67 shorter events, 0.4 us)
Async XLA Ops:
  9.4 10.2 %copy-start = (f32[1,5,8,32,128]{4,3,2,1,0:T(8,128)S(1)}, f32[1,5,8,32,128]{4,3,2,1,0:T(8,128)}, u32[]{:S(2)}) copy-start(f32[1,5,8,32,128]{4,3,2,1,0:T(8,128)} %param.7) | copy-start | bytes 1966084
  9.4 75.4 %all-to-all-start = ((f32[8,1,5,8,16,128]{5,4,3,2,1,0:T(8,128)}), f32[8,1,5,8,16,128]{5,4,3,2,1,0:T(8,128)S(1)}, u32[]{:S(2)}, u32[]{:S(2)}) async-start(f32[8,1,5,8,16,128]{5,4,3,2,1,0:T(8,128)} %stack.38), calls=%async_computation | async-start | bytes 5242880 | tf_op jit(solution)/shard_map/all_to_all | solution.py:16
  19.6 96.1 %reduce-scatter.2.cloned.1.call-start = ((), (), s32[]{:S(2)}) async-start(), calls=%async_computation.2 | async-start | bytes 2949120 | tf_op jit(solution)/shard_map/reduce_scatter | solution.py:92
  20.3 72.7 %collective-permute-start = (f32[1,5,1,32,128]{4,3,2,1,0:T(8,128)}, f32[1,5,1,32,128]{4,3,2,1,0:T(8,128)}, u32[]{:S(2)}, u32[]{:S(2)}) collective-permute-start(f32[1,5,1,32,128]{4,3,2,1,0:T(8,128)} %get-tuple-element.42), channel_id=1, source_target_pairs={{1,0},{2,1},{3,2},{4,3},{5,4},{6,5},{7,6},{8,7},{9,8},{10,9},{11,1... | collective-permute-start | bytes 245768 | tf_op jit(solution)/shard_map/ppermute | solution.py:27
  23.8 9.4 %copy-start.17 = (s32[1,2,8,128]{3,2,1,0:T(8,128)S(1)}, s32[1,2,8,128]{3,2,1,0:T(8,128)}, u32[]{:S(2)}) copy-start(s32[1,2,8,128]{3,2,1,0:T(8,128)} %param.13) | copy-start | bytes 24580
  23.8 69.2 %collective-permute-start.1 = (f32[1,5,1,32,128]{4,3,2,1,0:T(8,128)}, f32[1,5,1,32,128]{4,3,2,1,0:T(8,128)}, u32[]{:S(2)}, u32[]{:S(2)}) collective-permute-start(f32[1,5,1,32,128]{4,3,2,1,0:T(8,128)} %get-tuple-element.41), channel_id=1, source_target_pairs={{0,1},{1,2},{2,3},{3,4},{4,5},{5,6},{6,7},{7,8},{8,9},{9,10},{10,1... | collective-permute-start | bytes 245768 | tf_op jit(solution)/shard_map/ppermute | solution.py:24
  26.1 7.9 %copy-start.16 = (f32[8,32,128]{2,1,0:T(8,128)S(1)}, f32[8,32,128]{2,1,0:T(8,128)}, u32[]{:S(2)}) copy-start(f32[8,32,128]{2,1,0:T(8,128)} %param.9) | copy-start | bytes 393220
  26.1 17.4 %collective-permute-start.3 = (f32[1,5,8,16,128]{4,3,2,1,0:T(8,128)}, f32[1,5,8,16,128]{4,3,2,1,0:T(8,128)}, u32[]{:S(2)}, u32[]{:S(2)}) collective-permute-start(f32[1,5,8,16,128]{4,3,2,1,0:T(8,128)} %get-tuple-element.25), channel_id=1, source_target_pairs={{0,32},{32,0},{1,33},{33,1},{2,34},{34,2},{3,35},{35,3},{4,36},{36... | collective-permute-start | bytes 983048 | tf_op jit(solution)/shard_map/ppermute | solution.py:87
  30.7 12.9 %copy-start.7 = (f32[5,8,16,128]{3,2,1,0:T(8,128)S(1)}, f32[5,8,16,128]{3,2,1,0:T(8,128)}, u32[]{:S(2)}) copy-start(f32[5,8,16,128]{3,2,1,0:T(8,128)} %get-tuple-element.24) | copy-start | bytes 983044
  31.1 0.9 copy-start.3
  31.1 2.0 %copy-start.5 = (f32[1,5,8,32,127]{4,3,2,1,0:T(8,128)}, f32[1,5,8,32,127]{4,3,2,1,0:T(8,128)S(1)}, u32[]{:S(2)}) copy-start(f32[1,5,8,32,127]{4,3,2,1,0:T(8,128)S(1)} %get-tuple-element.48) | copy-start | bytes 1950724
  43.6 3.0 %copy-start.14 = (f32[3,5,5]{2,0,1:T(4,128)S(1)}, f32[3,5,5]{2,0,1:T(4,128)}, u32[]{:S(2)}) copy-start(f32[3,5,5]{2,0,1:T(4,128)} %param.11) | copy-start | bytes 904
  84.9 1.6 %copy-start.30 = (s32[2,8,128]{2,1,0:T(8,128)S(1)}, s32[2,8,128]{2,1,0:T(8,128)}, u32[]{:S(2)}) copy-start(s32[2,8,128]{2,1,0:T(8,128)} %param.12) | copy-start | bytes 24580
  84.9 3.0 %copy-start.12 = (f32[2,2,8,128,8]{3,4,2,1,0:T(8,128)S(1)}, f32[2,2,8,128,8]{3,4,2,1,0:T(8,128)}, u32[]{:S(2)}) copy-start(f32[2,2,8,128,8]{3,4,2,1,0:T(8,128)} %compare_convert_fusion) | copy-start | bytes 393220
  88.5 24.5 %copy-start.1 = (f32[1,5,8,31,128]{4,3,2,1,0:T(8,128)S(1)}, f32[1,5,8,31,128]{4,3,2,1,0:T(8,128)}, u32[]{:S(2)}) copy-start(f32[1,5,8,31,128]{4,3,2,1,0:T(8,128)} %get-tuple-element.43) | copy-start | bytes 1904644
  88.5 24.5 %copy-start.2 = (f32[1,5,8,31,128]{4,3,2,1,0:T(8,128)S(1)}, f32[1,5,8,31,128]{4,3,2,1,0:T(8,128)}, u32[]{:S(2)}) copy-start(f32[1,5,8,31,128]{4,3,2,1,0:T(8,128)} %get-tuple-element.44) | copy-start | bytes 1904644
  88.6 24.3 %collective-permute-start.2 = (f32[92160]{0:T(1024)S(1)}, f32[92160]{0:T(1024)S(1)}, u32[]{:S(2)}, u32[]{:S(2)}) collective-permute-start(f32[92160]{0:T(1024)S(1)} %pad_maximum_fusion.4), channel_id=1, source_target_pairs={{0,32},{32,0},{1,33},{33,1},{2,34},{34,2},{3,35},{35,3},{4,36},{36... | collective-permute-start | bytes 1105928 | tf_op jit(solution)/shard_map/ppermute | solution.py:109
  94.1 19.1 %copy-start.4 = (f32[1,5,8,32,127]{4,3,2,1,0:T(8,128)S(1)}, f32[1,5,8,32,127]{4,3,2,1,0:T(8,128)}, u32[]{:S(2)}) copy-start(f32[1,5,8,32,127]{4,3,2,1,0:T(8,128)} %copy-done.3) | copy-start | bytes 1950724
  94.1 19.1 %copy-start.6 = (f32[1,5,8,32,127]{4,3,2,1,0:T(8,128)S(1)}, f32[1,5,8,32,127]{4,3,2,1,0:T(8,128)}, u32[]{:S(2)}) copy-start(f32[1,5,8,32,127]{4,3,2,1,0:T(8,128)} %copy-done.5) | copy-start | bytes 1950724
  94.1 19.1 %copy-start.9 = (f32[8,32,128]{2,1,0:T(8,128)S(1)}, f32[8,32,128]{2,1,0:T(8,128)}, u32[]{:S(2)}) copy-start(f32[8,32,128]{2,1,0:T(8,128)} %get-tuple-element.38) | copy-start | bytes 393220
  94.1 19.1 %copy-start.10 = (f32[8,32,128]{2,1,0:T(8,128)S(1)}, f32[8,32,128]{2,1,0:T(8,128)}, u32[]{:S(2)}) copy-start(f32[8,32,128]{2,1,0:T(8,128)} %get-tuple-element.39) | copy-start | bytes 393220
  94.2 19.1 %copy-start.11 = (f32[8,32,128]{2,1,0:T(8,128)S(1)}, f32[8,32,128]{2,1,0:T(8,128)}, u32[]{:S(2)}) copy-start(f32[8,32,128]{2,1,0:T(8,128)} %get-tuple-element.40) | copy-start | bytes 393220
  94.2 19.1 %copy-start.15 = (f32[8,32,128]{2,1,0:T(8,128)S(1)}, f32[8,32,128]{2,1,0:T(8,128)}, u32[]{:S(2)}) copy-start(f32[8,32,128]{2,1,0:T(8,128)} %param.10) | copy-start | bytes 393220
  94.2 19.1 %copy-start.18 = (f32[5]{0:T(128)S(1)}, f32[5]{0:T(128)}, u32[]{:S(2)}) copy-start(f32[5]{0:T(128)} %get-tuple-element.8) | copy-start | bytes 64
  94.2 19.1 %copy-start.19 = (f32[5]{0:T(128)S(1)}, f32[5]{0:T(128)}, u32[]{:S(2)}) copy-start(f32[5]{0:T(128)} %get-tuple-element.9) | copy-start | bytes 64
  94.2 19.1 %copy-start.20 = (f32[5]{0:T(128)S(1)}, f32[5]{0:T(128)}, u32[]{:S(2)}) copy-start(f32[5]{0:T(128)} %get-tuple-element.10) | copy-start | bytes 64
  94.2 19.1 %copy-start.21 = (f32[5]{0:T(128)S(1)}, f32[5]{0:T(128)}, u32[]{:S(2)}) copy-start(f32[5]{0:T(128)} %get-tuple-element.11) | copy-start | bytes 64
  94.2 19.1 %copy-start.22 = (f32[5]{0:T(128)S(1)}, f32[5]{0:T(128)}, u32[]{:S(2)}) copy-start(f32[5]{0:T(128)} %get-tuple-element.12) | copy-start | bytes 64
  94.2 19.1 %copy-start.23 = (f32[5]{0:T(128)S(1)}, f32[5]{0:T(128)}, u32[]{:S(2)}) copy-start(f32[5]{0:T(128)} %get-tuple-element.13) | copy-start | bytes 64
  94.2 19.1 %copy-start.24 = (f32[5]{0:T(128)S(1)}, f32[5]{0:T(128)}, u32[]{:S(2)}) copy-start(f32[5]{0:T(128)} %get-tuple-element.14) | copy-start | bytes 64
  94.2 19.1 %copy-start.25 = (f32[5]{0:T(128)S(1)}, f32[5]{0:T(128)}, u32[]{:S(2)}) copy-start(f32[5]{0:T(128)} %get-tuple-element.15) | copy-start | bytes 64
  94.3 19.1 %copy-start.26 = (f32[5]{0:T(128)S(1)}, f32[5]{0:T(128)}, u32[]{:S(2)}) copy-start(f32[5]{0:T(128)} %get-tuple-element.16) | copy-start | bytes 64
  94.3 19.1 %copy-start.27 = (f32[5]{0:T(128)S(1)}, f32[5]{0:T(128)}, u32[]{:S(2)}) copy-start(f32[5]{0:T(128)} %get-tuple-element.17) | copy-start | bytes 64
  94.3 19.1 %copy-start.28 = (f32[5]{0:T(128)S(1)}, f32[5]{0:T(128)}, u32[]{:S(2)}) copy-start(f32[5]{0:T(128)} %get-tuple-element.18) | copy-start | bytes 64
  94.3 19.1 %copy-start.29 = (f32[5]{0:T(128)S(1)}, f32[5]{0:T(128)}, u32[]{:S(2)}) copy-start(f32[5]{0:T(128)} %get-tuple-element.19) | copy-start | bytes 64
  113.4 2.3 %copy-start.13 = (f32[8,32,128]{2,1,0:T(8,128)S(1)}, f32[8,32,128]{2,1,0:T(8,128)}, u32[]{:S(2)}) copy-start(f32[8,32,128]{2,1,0:T(8,128)} %broadcast_multiply_fusion) | copy-start | bytes 393220
  115.6 1.1 copy-start.8
Sparse Core Ops, SparseCore 0:
  46.7 59.4 reduce-scatter.1
